TPU v7x, 32 devices: a whole 2x2x4 slice. The times are simulated.
32 devices in a mesh: energy: 4 (over z), atom: 8 (over y, x, core).
Axes of the slice: x: 2, y: 2, z: 4, core: 2. Of those that a mesh axis runs over, the one named last changes fastest.
Arguments:
- t_mats: bfloat16 [4, 16, 2048], P('energy', 'atom'), may hold values from -0.75 to 0.75
- struct_table: bfloat16 [4, 64, 2048], P('energy'), may hold values from -0.359375 to 0.359375
- zone_atoms: int32 [16, 64], P('atom'), may hold values from 0 to 15, as said below
- zone_size: int32 [16], P('atom'), may hold values from 32 to 64
- pair_index: int32 [16, 384], P('atom'), may hold values from 0 to 63
- zone_link: int32 [16, 384], P('atom'), may hold values from 0 to 63
- weights: float32 [4, 2], P('energy'), may hold values from -1 to 1
Outputs:
- green: float32 [16, 2048], P('atom')
Inputs may be any that keep to these rules, and one draw needn't show every extreme that they name: Atom g is owned by index g // 2 of the atom axis; zone_atoms[g, 0] is g; the owner of every member of atom g's zone lies -4 to 3 steps from g's owner along the atom axis, counted around the axis, and both extreme offsets occur in every zone; members may repeat (periodic images).
All inputs are finite; a program needn't handle non-finite values.
Results may differ from a plain program's by a relative error of at most 0.003.
Values may be sent and summed in bfloat16 or wider, within the bound.
No kernel may reach another device: no remote copies, remote signals or barrier semaphores. Data moves between devices by JAX's collectives and lax.ppermute only.
A program may use at most 128 MiB of HBM per device.

v0:
```python
import jax
import jax.numpy as jnp
from jax import lax
from jax.sharding import PartitionSpec as P

L = 32
Z = 64
NB = 6
ITERS = 3


def real_form(block):
    parts = block.reshape(block.shape[:-1] + (2, L, L))
    real_part = parts[..., 0, :, :]
    imag_part = parts[..., 1, :, :]
    top_rows = jnp.concatenate([real_part, -imag_part], axis=-1)
    bottom_rows = jnp.concatenate([imag_part, real_part], axis=-1)
    return jnp.concatenate([top_rows, bottom_rows], axis=-2)


def scatter_terms(couplings, gathered, pattern):
    products = jnp.einsum(pattern, couplings, gathered, preferred_element_type=jnp.float32)
    real_part = products[..., 0, 0, :, :] - products[..., 1, 1, :, :]
    imag_part = products[..., 1, 0, :, :] + products[..., 0, 1, :, :]
    return jnp.concatenate([real_part, imag_part], axis=-2)


def take_links(column_parts, link_rows):
    return jax.vmap(
        lambda member_col, member_links: member_col[:, member_links], in_axes=(1, 0), out_axes=1
    )(column_parts, link_rows)


def solve_zones(zone_block, couplings_flat, links):
    e_dev, a_dev = (zone_block.shape[0], zone_block.shape[1])
    t_real = real_form(zone_block)
    couplings = couplings_flat.reshape(e_dev, a_dev, Z, NB, 2, L, L)
    start_block = t_real[:, :, 0, :, :L].astype(jnp.float32)
    start = jnp.zeros((e_dev, a_dev, Z, 2 * L, L), jnp.float32).at[:, :, 0].set(start_block)
    column = start
    for repeat in range(ITERS - 1):
        column_parts = column.astype(jnp.bfloat16).reshape(e_dev, a_dev, Z, 2, L, L)
        gathered = take_links(column_parts, links).reshape(e_dev, a_dev, Z, NB, 2, L, L)
        coupled = scatter_terms(couplings, gathered, "eganpij,eganqjk->egapqik").astype(
            jnp.bfloat16
        )
        column = (
            jnp.einsum("egaij,egajk->egaik", t_real, coupled, preferred_element_type=jnp.float32)
            + start
        )
    column_parts = column.astype(jnp.bfloat16).reshape(e_dev, a_dev, Z, 2, L, L)
    gathered = take_links(column_parts, links[:, :NB])
    coupled = scatter_terms(couplings[:, :, 0], gathered, "egnpij,egnqjk->egpqik").astype(
        jnp.bfloat16
    )
    return (
        jnp.einsum("egij,egjk->egik", t_real[:, :, 0], coupled, preferred_element_type=jnp.float32)
        + start_block
    )


def body(t_mats, struct_table, zone_atoms, zone_size, pair_index, zone_link, weights):
    e_dev, a_dev, block_flat = t_mats.shape
    window = lax.all_gather(t_mats, "atom", axis=1, tiled=True)
    present = jnp.arange(Z, dtype=jnp.int32)[None, :] < zone_size[:, None]
    zone_block = jnp.where(
        present[None, :, :, None], window[:, zone_atoms], jnp.zeros((), jnp.bfloat16)
    )
    couplings_flat = struct_table[:, pair_index]
    diagonal = solve_zones(zone_block, couplings_flat, zone_link)
    real_rows = diagonal[:, :, :L, :].reshape(e_dev, a_dev, L * L)
    imag_rows = diagonal[:, :, L:, :].reshape(e_dev, a_dev, L * L)
    w_real = weights[:, 0][:, None, None]
    w_imag = weights[:, 1][:, None, None]
    green_real = jnp.sum(w_real * real_rows - w_imag * imag_rows, axis=0)
    green_imag = jnp.sum(w_real * imag_rows + w_imag * real_rows, axis=0)
    local_green = jnp.concatenate([green_real, green_imag], axis=-1)
    return lax.psum(local_green, "energy")


def solution(mesh):
    return jax.shard_map(
        body,
        mesh=mesh,
        in_specs=(
            P("energy", "atom", None),
            P("energy", None, None),
            P("atom", None),
            P("atom"),
            P("atom", None),
            P("atom", None),
            P("energy", None),
        ),
        out_specs=P("atom", None),
        check_vma=False,
    )
```

profile of v0, /device:TPU:0, one launch (start us, length us, event | category | flops | bytes accessed | tf_op | source)
XLA Modules:
  0.0 153.0 jit_solution(8475652753170242469)
XLA Ops:
  0.8 10.7 %all_gather.3 = bf16[1,16,2048]{2,0,1:T(2,128)(2,1)S(1)} all-gather(bf16[1,2,2048]{2,0,1:T(2,128)(2,1)S(1)} %copy.91), channel_id=1, replica_groups=mesh['energy'=4,'atom'=8] {'atom'}, dimensions={1}, use_global_device_ids=true | all-gather | bytes 73728 | tf_op jit(solution)/shard_map/all_gather | solution.py:64
  13.9 2.0 %copy.93 = bf16[1,2,64,2,32,32]{5,4,2,1,3,0:T(8,128)(2,1)S(1)} copy(bf16[1,2,64,2,32,32]{2,1,5,4,3,0:T(2,128)(2,1)S(1)} %gather.18) | data formatting | bytes 1048576 | tf_op jit(solution)/shard_map/gather | solution.py:67
  19.3 9.2 %gather_fusion.2 = bf16[768,2,32,32]{3,2,1,0:T(8,128)(2,1)} fusion(bf16[2,64,2,32,32]{4,3,2,1,0:T(8,128)(2,1)S(1)} %bitcast.153, s32[768]{0:T(1024)S(1)} %reshape.305), kind=kCustom, calls=%fused_computation.2 | custom fusion | bytes 6297600 | tf_op jit(solution)/shard_map/vmap()/gather | solution.py:30
  28.5 3.4 %gather_fusion.1 = bf16[768,2048]{1,0:T(8,128)(2,1)S(1)} fusion(bf16[64,2048]{1,0:T(8,128)(2,1)S(1)} %bitcast.151, s32[1024]{0:T(1024)S(1)} %pad_clamp_fusion), kind=kCustom, calls=%fused_computation.1 | custom fusion | bytes 6294528 | tf_op jit(solution)/shard_map/gather | solution.py:69
  31.9 11.8 %reshape.277 = bf16[2,64,6,2,32,32]{5,4,3,2,1,0:T(8,128)(2,1)} reshape(bf16[768,2048]{1,0:T(8,128)(2,1)S(1)} %gather_fusion.1) | data formatting | bytes 6291456 | tf_op jit(solution)/shard_map/reshape.48
  43.7 17.2 %fusion.6 = f32[1,2,64,2,2,32,32]{5,6,3,4,2,1,0:T(8,128)} fusion(bf16[2,64,6,2,32,32,1]{5,4,3,2,1,0,6:T(8,128)(2,1)} %bitcast.155, bf16[2,64,6,2,32,32]{5,4,3,2,1,0:T(8,128)(2,1)} %reshape.277), kind=kOutput, calls=%fused_computation.11 | convolution fusion | flops 201326592 | bytes 8388608 | tf_op jit(solution)/shard_map/eganpij,eganqjk->egapqik/dot_general | solution.py:22
  60.9 2.7 %fusion.27 = bf16[2,64,32,32]{2,3,1,0:T(8,128)(2,1)S(1)} fusion(f32[1,2,64,2,2,32,32]{5,6,3,4,2,1,0:T(8,128)} %fusion.6), kind=kLoop, calls=%fused_computation.34 | loop fusion | flops 262144 | bytes 1310720 | tf_op jit(solution)/shard_map/sub | solution.py:23
  63.7 2.9 %fusion.28 = bf16[2,64,32,32]{2,3,1,0:T(8,128)(2,1)S(1)} fusion(f32[1,2,64,2,2,32,32]{5,6,3,4,2,1,0:T(8,128)} %fusion.6), kind=kLoop, calls=%fused_computation.35 | loop fusion | flops 262144 | bytes 1310720 | tf_op jit(solution)/shard_map/add | solution.py:24
  66.6 1.3 fusion.24
  67.9 1.3 copy-done.7
  70.0 1.8 %convert_element_type.37 = bf16[1,2,64,64,32]{3,4,2,1,0:T(8,128)(2,1)S(1)} convert(f32[1,2,64,64,32]{3,4,2,1,0:T(8,128)} %constant_dynamic-update-slice_fusion.1) | non-fusion elementwise | flops 262144 | bytes 1572864 | tf_op jit(solution)/shard_map/convert_element_type | solution.py:42
  73.0 9.4 %gather_fusion.3 = bf16[768,2,32,32]{3,2,1,0:T(8,128)(2,1)} fusion(bf16[2,64,2,32,32]{4,3,2,1,0:T(8,128)(2,1)S(1)} %bitcast.154, s32[768]{0:T(1024)S(1)} %reshape.305), kind=kCustom, calls=%fused_computation.3 | custom fusion | bytes 6297600 | tf_op jit(solution)/shard_map/vmap()/gather | solution.py:30
  82.4 17.2 %fusion.11 = f32[1,2,64,2,2,32,32]{5,6,3,4,2,1,0:T(8,128)} fusion(bf16[2,64,6,2,32,32,1]{5,4,3,2,1,0,6:T(8,128)(2,1)} %bitcast.156, bf16[2,64,6,2,32,32]{5,4,3,2,1,0:T(8,128)(2,1)} %reshape.277), kind=kOutput, calls=%fused_computation.12 | convolution fusion | flops 201326592 | bytes 8388608 | tf_op jit(solution)/shard_map/eganpij,eganqjk->egapqik/dot_general | solution.py:22
  99.6 2.7 %fusion.29 = bf16[2,64,32,32]{2,3,1,0:T(8,128)(2,1)S(1)} fusion(f32[1,2,64,2,2,32,32]{5,6,3,4,2,1,0:T(8,128)} %fusion.11), kind=kLoop, calls=%fused_computation.36 | loop fusion | flops 262144 | bytes 1310720 | tf_op jit(solution)/shard_map/sub | solution.py:23
  102.3 2.9 %fusion.30 = bf16[2,64,32,32]{2,3,1,0:T(8,128)(2,1)S(1)} fusion(f32[1,2,64,2,2,32,32]{5,6,3,4,2,1,0:T(8,128)} %fusion.11), kind=kLoop, calls=%fused_computation.37 | loop fusion | flops 262144 | bytes 1310720 | tf_op jit(solution)/shard_map/add | solution.py:24
  105.2 1.3 fusion.22
  106.5 1.3 copy-done.8
  108.6 2.8 %convert_element_type.38 = bf16[1,2,64,64,32]{3,4,2,1,0:T(8,128)(2,1)} convert(f32[1,2,64,64,32]{3,4,2,1,0:T(8,128)} %constant_dynamic-update-slice_fusion) | non-fusion elementwise | flops 262144 | bytes 1572864 | tf_op jit(solution)/shard_map/convert_element_type | solution.py:51
  111.4 2.9 %copy.134 = bf16[1,2,64,64,32]{4,3,2,1,0:T(8,128)(2,1)} copy(bf16[1,2,64,64,32]{3,4,2,1,0:T(8,128)(2,1)} %convert_element_type.38) | data formatting | bytes 1048576 | tf_op jit(solution)/shard_map/vmap()/transpose;reshape | solution.py:30
  114.4 2.9 %gather_fusion.4 = bf16[12,2,32,32]{3,2,1,0:T(8,128)(2,1)} fusion(bf16[2,64,2,32,32]{4,3,2,1,0:T(8,128)(2,1)} %bitcast.159, s32[12]{0:T(128)S(1)} %reshape.321), kind=kCustom, calls=%fused_computation.4 | custom fusion | bytes 98400 | tf_op jit(solution)/shard_map/vmap()/gather | solution.py:30
  117.4 11.6 %reshape.280 = bf16[1,2,64,6,2,32,32]{6,5,4,3,2,1,0:T(8,128)(2,1)} reshape(bf16[768,2048]{1,0:T(8,128)(2,1)S(1)} %copy-done.3) | data formatting | bytes 6291456 | tf_op jit(solution)/shard_map/reshape | solution.py:37
  129.0 1.3 convolution_bitcast_fusion
  132.0 1.2 multiply_subtract_fusion
  133.4 19.6 %psum.7 = f32[2,2048]{1,0:T(2,128)} all-reduce(f32[2,2048]{1,0:T(2,128)S(1)} %pad_maximum_fusion), channel_id=1, replica_groups=mesh['energy'=4,'atom'=8] {'energy'}, use_global_device_ids=true, to_apply=%region_0.1 | all-reduce | flops 4096 | bytes 32768 | tf_op jit(solution)/shard_map/psum | solution.py:78
  (64 shorter events, 11.3 us)
Async XLA Ops:
  0.0 28.5 %copy-start = (bf16[1,64,2048]{2,1,0:T(8,128)(2,1)S(1)}, bf16[1,64,2048]{2,1,0:T(8,128)(2,1)}, u32[]{:S(2)}) copy-start(bf16[1,64,2048]{2,1,0:T(8,128)(2,1)} %param.10) | copy-start | bytes 786436
  13.5 2.4 %copy-start.12 = (s32[2]{0:T(128)S(1)}, s32[2]{0:T(128)}, u32[]{:S(2)}) copy-start(s32[2]{0:T(128)} %param.12) | copy-start | bytes 28
  17.9 1.4 copy-start.4
  17.9 1.4 copy-start.9
  19.3 9.2 %copy-start.10 = (s32[2,384]{1,0:T(2,128)S(1)}, s32[2,384]{1,0:T(2,128)}, u32[]{:S(2)}) copy-start(s32[2,384]{1,0:T(2,128)} %param.13) | copy-start | bytes 9220
  31.9 11.8 %copy-start.2 = (bf16[768,2048]{1,0:T(8,128)(2,1)}, bf16[768,2048]{1,0:T(8,128)(2,1)S(1)}, u32[]{:S(2)}) copy-start(bf16[768,2048]{1,0:T(8,128)(2,1)S(1)} %gather_fusion.1) | copy-start | bytes 9437188
  63.7 2.9 %copy-start.5 = (bf16[1,2,64,64,64]{4,3,2,1,0:T(8,128)(2,1)S(1)}, bf16[1,2,64,64,64]{4,3,2,1,0:T(8,128)(2,1)}, u32[]{:S(2)}) copy-start(bf16[1,2,64,64,64]{4,3,2,1,0:T(8,128)(2,1)} %copy-done.4) | copy-start | bytes 3145732
  67.9 1.3 copy-start.7
  102.3 2.9 %copy-start.6 = (bf16[1,2,64,64,64]{4,3,2,1,0:T(8,128)(2,1)S(1)}, bf16[1,2,64,64,64]{4,3,2,1,0:T(8,128)(2,1)}, u32[]{:S(2)}) copy-start(bf16[1,2,64,64,64]{4,3,2,1,0:T(8,128)(2,1)} %copy-done.4) | copy-start | bytes 3145732
  106.5 1.3 copy-start.8
  111.4 5.9 %copy-start.3 = (bf16[768,2048]{1,0:T(8,128)(2,1)S(1)}, bf16[768,2048]{1,0:T(8,128)(2,1)}, u32[]{:S(2)}) copy-start(bf16[768,2048]{1,0:T(8,128)(2,1)} %copy-done.2) | copy-start | bytes 9437188
  117.3 14.0 %copy-start.11 = (f32[1,2]{1,0:T(1,128)S(1)}, f32[1,2]{1,0:T(1,128)}, u32[]{:S(2)}) copy-start(f32[1,2]{1,0:T(1,128)} %param.15) | copy-start | bytes 28
  117.3 35.6 %copy-start.1 = (bf16[1,64,2048]{2,1,0:T(8,128)(2,1)S(1)}, bf16[1,64,2048]{2,1,0:T(8,128)(2,1)}, u32[]{:S(2)}) copy-start(bf16[1,64,2048]{2,1,0:T(8,128)(2,1)} %param.10) | copy-start | bytes 786436
where the time goes:
time: 153 us
  local copies, waits for them, and re-layouts  63.7 us (42%)
  matrix products  39.3 us (26%)
  blocking collectives  30.3 us (20%)
  other arithmetic  19.4 us (13%)
    dot_general x3, matrix products, scatter_terms(): jnp.einsum(pattern, couplings, gathered, preferred_element_type=jnp.float32)  35.7 us
    gather x5, local copies, waits for them, and re-layouts, take_links(): member_col[:, member_links]  21.5 us
    psum x1, blocking collectives, body(): return lax.psum(local_green, 'energy')  19.6 us
    another operation x3, local copies, waits for them, and re-layouts  11.8 us
    reshape x1, local copies, waits for them, and re-layouts, solve_zones(): couplings = couplings_flat.reshape(e_dev, a_dev, Z, NB, 2, L, L)  11.6 us
    all_gather x1, blocking collectives, body(): window = lax.all_gather(t_mats, 'atom', axis=1, tiled=True)  10.7 us
    add x3, other arithmetic, scatter_terms(): imag_part = products[..., 1, 0, :, :] + products[..., 0, 1, :, :]  5.8 us
    sub x3, other arithmetic, scatter_terms(): real_part = products[..., 0, 0, :, :] - products[..., 1, 1, :, :]  5.49 us

commit v1 on v0

--- a/solution.py
+++ b/solution.py
@@ -7,6 +7,7 @@
 Z = 64
 NB = 6
 ITERS = 3
+pairs_all_end = lambda x0: jnp.sum(jax.lax.all_gather(x0, "energy"), 0)
 
 
 def real_form(block):
@@ -75,7 +76,7 @@
     green_real = jnp.sum(w_real * real_rows - w_imag * imag_rows, axis=0)
     green_imag = jnp.sum(w_real * imag_rows + w_imag * real_rows, axis=0)
     local_green = jnp.concatenate([green_real, green_imag], axis=-1)
-    return lax.psum(local_green, "energy")
+    return pairs_all_end(local_green)
 
 
 def solution(mesh):

time: 153 us -> 148 us (0.967)
  blocking collectives: 30.3 us -> 24 us
    psum x1 -> x0, blocking collectives: 19.6 us -> none  [body(): return lax.psum(local_green, 'energy')]
    all_gather x0 -> x1, blocking collectives: none -> 13.3 us  [pairs_all_end = lambda x0: jnp.sum(jax.lax.all_gather(x0, 'energy'), 0)]
where the time goes in v1:
time: 148 us; the launch traced here: 147 us
  local copies, waits for them, and re-layouts  63.7 us (43%)
  matrix products  39.3 us (27%)
  blocking collectives  24 us (16%)
  other arithmetic  20.1 us (14%)
    dot_general x3, matrix products, scatter_terms(): jnp.einsum(pattern, couplings, gathered, preferred_element_type=jnp.float32)  35.7 us
    gather x5, local copies, waits for them, and re-layouts, take_links(): member_col[:, member_links]  21.5 us
    all_gather x1, blocking collectives, pairs_all_end = lambda x0: jnp.sum(jax.lax.all_gather(x0, 'energy'), 0)  13.3 us
    another operation x3, local copies, waits for them, and re-layouts  11.8 us
    reshape x1, local copies, waits for them, and re-layouts, solve_zones(): couplings = couplings_flat.reshape(e_dev, a_dev, Z, NB, 2, L, L)  11.6 us
    all_gather x1, blocking collectives, body(): window = lax.all_gather(t_mats, 'atom', axis=1, tiled=True)  10.7 us
    add x3, other arithmetic, scatter_terms(): imag_part = products[..., 1, 0, :, :] + products[..., 0, 1, :, :]  5.8 us
    sub x3, other arithmetic, scatter_terms(): real_part = products[..., 0, 0, :, :] - products[..., 1, 1, :, :]  5.49 us

profile of v1, /device:TPU:0, one launch (start us, length us, event | category | flops | bytes accessed | tf_op | source)
XLA Modules:
  0.0 147.4 jit_solution(8224166855393187632)
XLA Ops:
  0.8 10.7 %all_gather.9 = bf16[1,16,2048]{2,0,1:T(2,128)(2,1)S(1)} all-gather(bf16[1,2,2048]{2,0,1:T(2,128)(2,1)S(1)} %copy.91), channel_id=1, replica_groups=mesh['energy'=4,'atom'=8] {'atom'}, dimensions={1}, use_global_device_ids=true | all-gather | bytes 73728 | tf_op jit(solution)/shard_map/all_gather | solution.py:65
  13.9 2.0 %copy.93 = bf16[1,2,64,2,32,32]{5,4,2,1,3,0:T(8,128)(2,1)S(1)} copy(bf16[1,2,64,2,32,32]{2,1,5,4,3,0:T(2,128)(2,1)S(1)} %gather.18) | data formatting | bytes 1048576 | tf_op jit(solution)/shard_map/gather | solution.py:68
  19.3 9.2 %gather_fusion.2 = bf16[768,2,32,32]{3,2,1,0:T(8,128)(2,1)} fusion(bf16[2,64,2,32,32]{4,3,2,1,0:T(8,128)(2,1)S(1)} %bitcast.155, s32[768]{0:T(1024)S(1)} %reshape.305), kind=kCustom, calls=%fused_computation.2 | custom fusion | bytes 6297600 | tf_op jit(solution)/shard_map/vmap()/gather | solution.py:31
  28.5 3.4 %gather_fusion.1 = bf16[768,2048]{1,0:T(8,128)(2,1)S(1)} fusion(bf16[64,2048]{1,0:T(8,128)(2,1)S(1)} %bitcast.153, s32[1024]{0:T(1024)S(1)} %pad_clamp_fusion), kind=kCustom, calls=%fused_computation.1 | custom fusion | bytes 6294528 | tf_op jit(solution)/shard_map/gather | solution.py:70
  31.9 11.8 %reshape.277 = bf16[2,64,6,2,32,32]{5,4,3,2,1,0:T(8,128)(2,1)} reshape(bf16[768,2048]{1,0:T(8,128)(2,1)S(1)} %gather_fusion.1) | data formatting | bytes 6291456 | tf_op jit(solution)/shard_map/reshape.48
  43.7 17.2 %fusion.6 = f32[1,2,64,2,2,32,32]{5,6,3,4,2,1,0:T(8,128)} fusion(bf16[2,64,6,2,32,32,1]{5,4,3,2,1,0,6:T(8,128)(2,1)} %bitcast.157, bf16[2,64,6,2,32,32]{5,4,3,2,1,0:T(8,128)(2,1)} %reshape.277), kind=kOutput, calls=%fused_computation.11 | convolution fusion | flops 201326592 | bytes 8388608 | tf_op jit(solution)/shard_map/eganpij,eganqjk->egapqik/dot_general | solution.py:23
  60.9 2.7 %fusion.27 = bf16[2,64,32,32]{2,3,1,0:T(8,128)(2,1)S(1)} fusion(f32[1,2,64,2,2,32,32]{5,6,3,4,2,1,0:T(8,128)} %fusion.6), kind=kLoop, calls=%fused_computation.34 | loop fusion | flops 262144 | bytes 1310720 | tf_op jit(solution)/shard_map/sub | solution.py:24
  63.7 2.9 %fusion.28 = bf16[2,64,32,32]{2,3,1,0:T(8,128)(2,1)S(1)} fusion(f32[1,2,64,2,2,32,32]{5,6,3,4,2,1,0:T(8,128)} %fusion.6), kind=kLoop, calls=%fused_computation.35 | loop fusion | flops 262144 | bytes 1310720 | tf_op jit(solution)/shard_map/add | solution.py:25
  66.6 1.3 fusion.24
  67.9 1.3 copy-done.7
  70.0 1.8 %convert_element_type.37 = bf16[1,2,64,64,32]{3,4,2,1,0:T(8,128)(2,1)S(1)} convert(f32[1,2,64,64,32]{3,4,2,1,0:T(8,128)} %constant_dynamic-update-slice_fusion.1) | non-fusion elementwise | flops 262144 | bytes 1572864 | tf_op jit(solution)/shard_map/convert_element_type | solution.py:43
  73.0 9.4 %gather_fusion.3 = bf16[768,2,32,32]{3,2,1,0:T(8,128)(2,1)} fusion(bf16[2,64,2,32,32]{4,3,2,1,0:T(8,128)(2,1)S(1)} %bitcast.156, s32[768]{0:T(1024)S(1)} %reshape.305), kind=kCustom, calls=%fused_computation.3 | custom fusion | bytes 6297600 | tf_op jit(solution)/shard_map/vmap()/gather | solution.py:31
  82.4 17.2 %fusion.11 = f32[1,2,64,2,2,32,32]{5,6,3,4,2,1,0:T(8,128)} fusion(bf16[2,64,6,2,32,32,1]{5,4,3,2,1,0,6:T(8,128)(2,1)} %bitcast.158, bf16[2,64,6,2,32,32]{5,4,3,2,1,0:T(8,128)(2,1)} %reshape.277), kind=kOutput, calls=%fused_computation.12 | convolution fusion | flops 201326592 | bytes 8388608 | tf_op jit(solution)/shard_map/eganpij,eganqjk->egapqik/dot_general | solution.py:23
  99.6 2.7 %fusion.29 = bf16[2,64,32,32]{2,3,1,0:T(8,128)(2,1)S(1)} fusion(f32[1,2,64,2,2,32,32]{5,6,3,4,2,1,0:T(8,128)} %fusion.11), kind=kLoop, calls=%fused_computation.36 | loop fusion | flops 262144 | bytes 1310720 | tf_op jit(solution)/shard_map/sub | solution.py:24
  102.3 2.9 %fusion.30 = bf16[2,64,32,32]{2,3,1,0:T(8,128)(2,1)S(1)} fusion(f32[1,2,64,2,2,32,32]{5,6,3,4,2,1,0:T(8,128)} %fusion.11), kind=kLoop, calls=%fused_computation.37 | loop fusion | flops 262144 | bytes 1310720 | tf_op jit(solution)/shard_map/add | solution.py:25
  105.2 1.3 fusion.22
  106.5 1.3 copy-done.8
  108.6 2.8 %convert_element_type.38 = bf16[1,2,64,64,32]{3,4,2,1,0:T(8,128)(2,1)} convert(f32[1,2,64,64,32]{3,4,2,1,0:T(8,128)} %constant_dynamic-update-slice_fusion) | non-fusion elementwise | flops 262144 | bytes 1572864 | tf_op jit(solution)/shard_map/convert_element_type | solution.py:52
  111.4 2.9 %copy.134 = bf16[1,2,64,64,32]{4,3,2,1,0:T(8,128)(2,1)} copy(bf16[1,2,64,64,32]{3,4,2,1,0:T(8,128)(2,1)} %convert_element_type.38) | data formatting | bytes 1048576 | tf_op jit(solution)/shard_map/vmap()/transpose;reshape | solution.py:31
  114.4 2.9 %gather_fusion.4 = bf16[12,2,32,32]{3,2,1,0:T(8,128)(2,1)} fusion(bf16[2,64,2,32,32]{4,3,2,1,0:T(8,128)(2,1)} %bitcast.161, s32[12]{0:T(128)S(1)} %reshape.321), kind=kCustom, calls=%fused_computation.4 | custom fusion | bytes 98400 | tf_op jit(solution)/shard_map/vmap()/gather | solution.py:31
  117.4 11.6 %reshape.280 = bf16[1,2,64,6,2,32,32]{6,5,4,3,2,1,0:T(8,128)(2,1)} reshape(bf16[768,2048]{1,0:T(8,128)(2,1)S(1)} %copy-done.3) | data formatting | bytes 6291456 | tf_op jit(solution)/shard_map/reshape | solution.py:38
  129.0 1.3 convolution_bitcast_fusion
  132.0 1.2 multiply_subtract_fusion
  133.4 13.3 %all-gather.1 = f32[4,2,2048]{2,1,0:T(2,128)S(1)} all-gather(f32[1,2,2048]{2,1,0:T(2,128)S(1)} %maximum_bitcast_fusion), channel_id=2, replica_groups=mesh['energy'=4,'atom'=8] {'energy'}, dimensions={0}, use_global_device_ids=true | all-gather | bytes 81920 | tf_op jit(solution)/shard_map/all_gather | solution.py:10
  (65 shorter events, 11.9 us)
Async XLA Ops:
  0.0 28.5 %copy-start = (bf16[1,64,2048]{2,1,0:T(8,128)(2,1)S(1)}, bf16[1,64,2048]{2,1,0:T(8,128)(2,1)}, u32[]{:S(2)}) copy-start(bf16[1,64,2048]{2,1,0:T(8,128)(2,1)} %param.10) | copy-start | bytes 786436
  13.5 2.4 %copy-start.12 = (s32[2]{0:T(128)S(1)}, s32[2]{0:T(128)}, u32[]{:S(2)}) copy-start(s32[2]{0:T(128)} %param.12) | copy-start | bytes 28
  17.9 1.4 copy-start.4
  17.9 1.4 copy-start.9
  19.3 9.2 %copy-start.10 = (s32[2,384]{1,0:T(2,128)S(1)}, s32[2,384]{1,0:T(2,128)}, u32[]{:S(2)}) copy-start(s32[2,384]{1,0:T(2,128)} %param.13) | copy-start | bytes 9220
  31.9 11.8 %copy-start.2 = (bf16[768,2048]{1,0:T(8,128)(2,1)}, bf16[768,2048]{1,0:T(8,128)(2,1)S(1)}, u32[]{:S(2)}) copy-start(bf16[768,2048]{1,0:T(8,128)(2,1)S(1)} %gather_fusion.1) | copy-start | bytes 9437188
  63.7 2.9 %copy-start.5 = (bf16[1,2,64,64,64]{4,3,2,1,0:T(8,128)(2,1)S(1)}, bf16[1,2,64,64,64]{4,3,2,1,0:T(8,128)(2,1)}, u32[]{:S(2)}) copy-start(bf16[1,2,64,64,64]{4,3,2,1,0:T(8,128)(2,1)} %copy-done.4) | copy-start | bytes 3145732
  67.9 1.3 copy-start.7
  102.3 2.9 %copy-start.6 = (bf16[1,2,64,64,64]{4,3,2,1,0:T(8,128)(2,1)S(1)}, bf16[1,2,64,64,64]{4,3,2,1,0:T(8,128)(2,1)}, u32[]{:S(2)}) copy-start(bf16[1,2,64,64,64]{4,3,2,1,0:T(8,128)(2,1)} %copy-done.4) | copy-start | bytes 3145732
  106.5 1.3 copy-start.8
  111.4 5.9 %copy-start.3 = (bf16[768,2048]{1,0:T(8,128)(2,1)S(1)}, bf16[768,2048]{1,0:T(8,128)(2,1)}, u32[]{:S(2)}) copy-start(bf16[768,2048]{1,0:T(8,128)(2,1)} %copy-done.2) | copy-start | bytes 9437188
  117.3 14.0 %copy-start.11 = (f32[1,2]{1,0:T(1,128)S(1)}, f32[1,2]{1,0:T(1,128)}, u32[]{:S(2)}) copy-start(f32[1,2]{1,0:T(1,128)} %param.15) | copy-start | bytes 28
  117.3 30.0 %copy-start.1 = (bf16[1,64,2048]{2,1,0:T(8,128)(2,1)S(1)}, bf16[1,64,2048]{2,1,0:T(8,128)(2,1)}, u32[]{:S(2)}) copy-start(bf16[1,64,2048]{2,1,0:T(8,128)(2,1)} %param.10) | copy-start | bytes 786436
